TPU v7x, 256 devices: a whole 4x4x8 slice. The times are simulated.
256 devices in a mesh: ctx: 32 (over z, y_hi, core), mp: 8 (over x, y_lo).
Axes of the slice: x: 4, y: 4 (y_hi: 2, y_lo: 2; y = y_hi * 2 + y_lo), z: 8, core: 2. Of those that a mesh axis runs over, the one named last changes fastest.
Arguments:
- proj: bfloat16 [8192, 3, 8192], P(('ctx', 'mp')), may hold values from -6 to 6
- conv_weight: float32 [3, 7, 8192], replicated, may hold values from -2 to 2
- residues: float32 [128, 16], P('mp'), may hold values from -1.5 to 1.5
- decays: float32 [128, 16], P('mp'), may hold values from 1.2207031e-05 to 0.03
- doc_lengths: int32 [64], replicated, may hold values from 1 to 768, 8192 in all
Outputs:
- mixed: bfloat16 [8192, 8192], P(('ctx', 'mp'))
All inputs are finite; a program needn't handle non-finite values.
Results may differ from a plain program's by a relative error of at most 0.014.
Values may be sent and summed in bfloat16 or wider, within the bound.
No kernel may reach another device: no remote copies, remote signals or barrier semaphores. Data moves between devices by JAX's collectives and lax.ppermute only.
A program may use at most 64 MiB of HBM per device.

v0:
```python
import jax
import jax.numpy as jnp
from jax import lax
from jax.sharding import PartitionSpec as P


def shifted_2(block, axis, distance):
    devices = range(lax.axis_size(axis))
    route = [(i - distance, i) for i in devices if i - distance in devices]
    return lax.ppermute(block, axis, route)


def document_number_index(doc_lengths, positions):
    doc_starts = jnp.cumsum(doc_lengths) - doc_lengths
    inside = (doc_starts[None, :] <= positions[:, None]).astype(jnp.int32)
    return jnp.sum(inside, axis=1) - 1


def short_convolution(padded, conv_weight, padded_document_ids, padded_pos, out_rows):
    kernel_len = conv_weight.shape[1]
    result = jnp.zeros((out_rows,) + padded.shape[1:], jnp.float32)
    own_docs = padded_document_ids[kernel_len - 1 :]
    for position_shift in range(kernel_len):
        begin_row = kernel_len - 1 - position_shift
        earlier = padded[begin_row : begin_row + out_rows].astype(jnp.float32)
        keep_mask = (padded_document_ids[begin_row : begin_row + out_rows] == own_docs) & (
            padded_pos[begin_row : begin_row + out_rows] >= 0
        )
        result = (
            result
            + conv_weight[:, position_shift, :][None]
            * earlier
            * keep_mask.astype(jnp.float32)[:, None, None]
        )
    return result


def filter_tile(coefficient, decays, out_index, piece_start, width_in):
    span = float(width_in)
    out_float = (out_index - piece_start).astype(jnp.float32)
    shifted = jnp.maximum(out_float - span, -span)
    left_neighbor = coefficient[:, :, None] * jnp.exp(-decays[:, :, None] * shifted[None, None, :])
    in_offsets = jnp.arange(width_in).astype(jnp.float32)
    right_neighbor = jnp.exp(-decays[:, :, None] * (span - in_offsets)[None, None, :])
    token_tile_rows = jnp.einsum(
        "ejz,ejx->ezx", left_neighbor, right_neighbor, precision=lax.Precision.HIGHEST
    )
    lag_matrix = (out_index - piece_start)[:, None] - jnp.arange(width_in, dtype=jnp.int32)[None, :]
    return jnp.where((lag_matrix >= 0)[None], token_tile_rows, 0.0)


def split_product(form, weights, inputs):
    upper_part = weights.astype(jnp.bfloat16)
    lower_part = (weights - upper_part.astype(jnp.float32)).astype(jnp.bfloat16)
    first = jnp.einsum(form, upper_part, inputs, preferred_element_type=jnp.float32)
    return first + jnp.einsum(form, lower_part, inputs, preferred_element_type=jnp.float32)


def long_filter(product, residues, decays, block_begin_position):
    block_len = product.shape[0]
    channels = product.shape[1]
    group_count = residues.shape[0]
    group_width = channels // group_count
    coefficient = residues * jnp.sqrt(decays)
    out_index = block_begin_position + jnp.arange(block_len, dtype=jnp.int32)

    def one_tile(running, rows_part, part_start):
        width_in = rows_part.shape[0]
        token_tile_rows = filter_tile(coefficient, decays, out_index, part_start, width_in)
        inputs = rows_part.reshape(width_in, group_count, group_width)
        return running + split_product("grs,sgc->rgc", token_tile_rows, inputs)

    initial = jnp.zeros((block_len, group_count, group_width), jnp.float32)
    piece_rows = lax.all_gather(product, "ctx", axis=0, tiled=True)
    width_in = piece_rows.shape[0]
    count_blocks = width_in // block_len
    stacked = piece_rows.reshape(count_blocks, block_len, channels)
    starts = block_len * jnp.arange(count_blocks, dtype=jnp.int32)

    def scan_step(carry, pair):
        return (one_tile(carry, pair[0], pair[1]), None)

    result, unused = lax.scan(scan_step, initial, (stacked, starts))
    return result.reshape(block_len, channels).astype(jnp.bfloat16)


def shards(proj, conv_weight, residues, decays, doc_lengths):
    kernel_len = conv_weight.shape[1]
    channel_rows = lax.all_to_all(proj, "mp", split_axis=2, concat_axis=0, tiled=True)
    block_len = channel_rows.shape[0]
    channels = channel_rows.shape[2]
    local_weight = lax.dynamic_slice_in_dim(
        conv_weight, lax.axis_index("mp") * channels, channels, 2
    )
    tail_rows = shifted_2(channel_rows[block_len - (kernel_len - 1) :], "ctx", 1)
    block_begin_position = lax.axis_index("ctx") * block_len
    padded_pos = (
        block_begin_position
        - (kernel_len - 1)
        + jnp.arange(block_len + kernel_len - 1, dtype=jnp.int32)
    )
    padded_document_ids = document_number_index(doc_lengths, padded_pos)
    padded = jnp.concatenate([tail_rows, channel_rows], axis=0)
    conv = short_convolution(padded, local_weight, padded_document_ids, padded_pos, block_len)
    query_part = conv[:, 0]
    product = (conv[:, 1] * conv[:, 2]).astype(jnp.bfloat16)
    filtered = long_filter(product, residues, decays, block_begin_position)
    mixed_out = (query_part * filtered.astype(jnp.float32)).astype(jnp.bfloat16)
    return lax.all_to_all(mixed_out, "mp", split_axis=0, concat_axis=1, tiled=True)


def solution(mesh):
    return jax.shard_map(
        shards,
        mesh=mesh,
        in_specs=(P(("ctx", "mp"), None, None), P(), P("mp", None), P("mp", None), P()),
        out_specs=P(("ctx", "mp"), None),
        check_vma=False,
    )
```

profile of v0, /device:TPU:8, one launch (start us, length us, event | category | flops | bytes accessed | tf_op | source)
XLA Modules:
  0.0 531.1 jit_solution(9122464082286298592)
XLA Ops:
  6.5 10.6 %copy.23 = bf16[32,3,8192]{0,1,2:T(4,128)(2,1)} copy(bf16[32,3,8192]{2,0,1:T(8,128)(2,1)} %param.7) | data formatting | bytes 3145728 | tf_op args[0]
  17.2 9.8 %reshape.117 = bf16[8,2,49152]{2,1,0:T(2,128)(2,1)} reshape(bf16[8192,3,32]{2,1,0:T(4,128)(2,1)} %bitcast.54) | data formatting | bytes 3145728
  27.0 5.9 %all-to-all-start = ((bf16[8,2,49152]{2,1,0:T(2,128)(2,1)}), bf16[8,2,49152]{2,1,0:T(2,128)(2,1)S(1)}, u32[]{:S(2)}, u32[]{:S(2)}) async-start(bf16[8,2,49152]{2,1,0:T(2,128)(2,1)} %reshape.117), calls=%async_computation | async-start | bytes 3145728 | tf_op jit(solution)/shard_map/all_to_all | solution.py:89
  33.3 1.6 constant_dynamic-slice_fusion.6
  35.0 19.6 %all-to-all-done = bf16[8,2,49152]{2,1,0:T(2,128)(2,1)S(1)} async-done(((bf16[8,2,49152]{2,1,0:T(2,128)(2,1)}), bf16[8,2,49152]{2,1,0:T(2,128)(2,1)S(1)}, u32[]{:S(2)}, u32[]{:S(2)}) %all-to-all-start) | async-done | bytes 1572896 | tf_op jit(solution)/shard_map/all_to_all | solution.py:89
  54.7 7.6 %reshape.118 = bf16[8192,3,32]{2,1,0:T(4,128)(2,1)} reshape(bf16[8,2,49152]{2,1,0:T(2,128)(2,1)S(1)} %all-to-all-done) | data formatting | bytes 3145728
  62.3 10.5 %copy.31 = bf16[32,3,8,1024]{3,0,2,1:T(8,128)(2,1)S(1)} copy(bf16[32,3,8,1024]{0,1,3,2:T(4,128)(2,1)} %bitcast.53) | data formatting | bytes 3145728 | tf_op jit(solution)/shard_map/all_to_all | solution.py:89
  72.8 1.5 collective-permute-start
  75.0 3.9 multiply_add_fusion
  78.9 1.4 fusion.28
  80.4 142.8 %all-gather.3.cloned.1.call-done = bf16[8192,1,1024]{2,0,1:T(8,128)(2,1)} async-done(((bf16[256,1,1024]{2,0,1:T(8,128)(2,1)}), bf16[8192,1,1024]{2,0,1:T(8,128)(2,1)}) %all-gather.3.cloned.1.call-update) | async-done | bytes 16777232 | tf_op jit(solution)/shard_map/all_gather | solution.py:74
  223.1 282.1 %while.13 = (s32[]{:T(128)}, f32[256,16,64]{0,2,1:T(8,128)S(1)}, bf16[32,256,1024]{2,1,0:T(8,128)(2,1)}, s32[32]{0:T(128)S(1)}, f32[16,16]{1,0:T(8,128)S(1)}, /*...) while((s32[]{:T(128)}, f32[256,16,64]{0,2,1:T(8,128)S(1)}, ...), condition=%wide.region_3.4_spmd.clone, body=%wide.region_2.3_spmd.clone.sunk | while | flops 477169920 | bytes 20127888 | solution.py:83
  225.2 1.1 constant_dynamic-slice_fusion.9
  226.4 3.7 fusion.42
  234.0 1.1 constant_dynamic-slice_fusion.9
  235.3 3.7 fusion.42
  242.8 1.1 constant_dynamic-slice_fusion.9
  244.1 3.7 fusion.42
  251.6 1.1 constant_dynamic-slice_fusion.9
  252.9 3.7 fusion.42
  261.7 3.7 fusion.42
  270.5 3.7 fusion.42
  279.3 3.7 fusion.42
  288.2 3.7 fusion.42
  295.7 1.1 constant_dynamic-slice_fusion.9
  297.0 3.7 fusion.42
  304.5 1.1 constant_dynamic-slice_fusion.9
  305.8 3.7 fusion.42
  313.3 1.1 constant_dynamic-slice_fusion.9
  314.6 3.7 fusion.42
  322.1 1.1 constant_dynamic-slice_fusion.9
  323.4 3.7 fusion.42
  331.0 1.1 constant_dynamic-slice_fusion.9
  332.2 3.7 fusion.42
  341.1 3.7 fusion.42
  349.9 3.7 fusion.42
  358.7 3.7 fusion.42
  367.5 3.7 fusion.42
  375.0 1.1 constant_dynamic-slice_fusion.9
  376.3 3.7 fusion.42
  383.9 1.1 constant_dynamic-slice_fusion.9
  385.1 3.7 fusion.42
  392.7 1.1 constant_dynamic-slice_fusion.9
  394.0 3.7 fusion.42
  401.5 1.1 constant_dynamic-slice_fusion.9
  402.8 3.7 fusion.42
  410.3 1.1 constant_dynamic-slice_fusion.9
  411.6 3.7 fusion.42
  419.1 1.1 constant_dynamic-slice_fusion.9
  420.4 3.7 fusion.42
  429.2 3.7 fusion.42
  438.1 3.7 fusion.42
  446.9 3.7 fusion.42
  455.7 3.7 fusion.42
  463.2 1.1 constant_dynamic-slice_fusion.9
  464.5 3.7 fusion.42
  472.0 1.1 constant_dynamic-slice_fusion.9
  473.3 3.7 fusion.42
  482.1 3.7 fusion.42
  491.0 3.7 fusion.42
  499.8 3.7 fusion.42
  505.4 1.3 copy.28
  507.2 1.4 multiply_convert_fusion
  508.6 14.8 %all_to_all.34 = bf16[8,32,1024]{2,1,0:T(8,128)(2,1)S(1)} all-to-all(bf16[8,32,1024]{2,1,0:T(8,128)(2,1)S(1)} %multiply_convert_fusion), channel_id=1, replica_groups=mesh['ctx'=32,'mp'=8] {'mp'}, dimensions={0} | all-to-all | bytes 1048576 | tf_op jit(solution)/shard_map/all_to_all | solution.py:109
  (268 shorter events, 144.9 us)
Async XLA Ops:
  27.0 5.9 %copy-start.2 = (s32[64]{0:T(128)S(1)}, s32[64]{0:T(128)}, u32[]{:S(2)}) copy-start(s32[64]{0:T(128)} %param.11) | copy-start | bytes 772
  27.0 27.7 %all-to-all-start = ((bf16[8,2,49152]{2,1,0:T(2,128)(2,1)}), bf16[8,2,49152]{2,1,0:T(2,128)(2,1)S(1)}, u32[]{:S(2)}, u32[]{:S(2)}) async-start(bf16[8,2,49152]{2,1,0:T(2,128)(2,1)} %reshape.117), calls=%async_computation | async-start | bytes 3145728 | tf_op jit(solution)/shard_map/all_to_all | solution.py:89
  32.8 190.3 %all-gather.3.cloned.1.call-start = ((), (), s32[]{:S(2)}) async-start(), calls=%async_computation.2 | async-start | bytes 17301504 | tf_op jit(solution)/shard_map/all_gather | solution.py:74
  72.8 2.2 collective-permute-start
  78.9 1.4 copy-start
  78.9 1.4 copy-start.1
Sparse Core Ops, SparseCore 0:
  80.4 142.6 all-gather.2
where the time goes:
time: 534 us; the launch traced here: 531 us
  matrix products  175 us (33%)
  waiting for transfers between devices  163 us (31%)
  local copies, waits for them, and re-layouts  103 us (19%)
  other arithmetic  52.4 us (10%)
  blocking collectives  14.8 us (3%)
  between operations  13.6 us (3%)
  starting transfers between devices  7.36 us (1%)
    all_gather x1, waiting for transfers between devices, long_filter(): piece_rows = lax.all_gather(product, 'ctx', axis=0, tiled=True)  143 us
    dot_general x32, matrix products, filter_tile(): jnp.einsum('ejz,ejx->ezx', left_neighbor, right_neighbor, precision=lax.P...  119 us
    dynamic_slice x96, local copies, waits for them, and re-layouts, long_filter(): result, unused = lax.scan(scan_step, initial, (stacked, starts))  59.9 us
    dot_general x32, matrix products, split_product(): jnp.einsum(form, lower_part, inputs, preferred_element_type=jnp.float32)  31.6 us
    unnamed x13, local copies, waits for them, and re-layouts  28.1 us
    dot_general x32, matrix products, split_product(): jnp.einsum(form, upper_part, inputs, preferred_element_type=jnp.float32)  23.8 us
    sub x32, other arithmetic, filter_tile(): span - in_offsets  20.9 us
    sub x32, other arithmetic, filter_tile(): out_index - piece_start  20.7 us
  transfers between devices with their start and end apart: 3, of which 3 were waited for; matrix products, arithmetic and copies ran while one was open for 0% of the time, Pallas kernels for 0%

commit v1 on v0

--- a/solution.py
+++ b/solution.py
@@ -71,7 +71,10 @@
         return running + split_product("grs,sgc->rgc", token_tile_rows, inputs)
 
     initial = jnp.zeros((block_len, group_count, group_width), jnp.float32)
-    piece_rows = lax.all_gather(product, "ctx", axis=0, tiled=True)
+    heard = tuple((product for _ in range(jax.lax.axis_size("ctx"))))
+    arr_now = jnp.stack(heard)
+    u_next = jax.lax.all_to_all(arr_now, axis_name="ctx", split_axis=0, concat_axis=0)
+    piece_rows = jnp.concatenate(u_next, axis=0)
     width_in = piece_rows.shape[0]
     count_blocks = width_in // block_len
     stacked = piece_rows.reshape(count_blocks, block_len, channels)

time: 534 us -> 845 us (1.58); the launches traced: 531 us -> 833 us
  waiting for transfers between devices: 163 us -> 379 us
  matrix products: 175 us -> 243 us
  starting transfers between devices: 7.36 us -> 23.3 us
  local copies, waits for them, and re-layouts: 103 us -> 117 us
  between operations: 13.6 us -> 0.18 us
    all_to_all x0 -> x1, waiting for transfers between devices: none -> 358 us  [long_filter(): jax.lax.all_to_all(arr_now, axis_name='ctx', split_axis=0, concat_axis=0)]
    all_gather x1 -> x0, waiting for transfers between devices: 143 us -> none  [long_filter(): piece_rows = lax.all_gather(product, 'ctx', axis=0, tiled=True)]
    dot_general x32, matrix products: 31.6 us -> 100 us  [split_product(): jnp.einsum(form, lower_part, inputs, preferred_element_type=jnp.float32)]
    all_to_all x0 -> x1, starting transfers between devices: none -> 16.2 us  [long_filter(): jax.lax.all_to_all(arr_now, axis_name='ctx', split_axis=0, concat_axis=0)]
    dynamic_slice x96 -> x64, local copies, waits for them, and re-layouts: 59.9 us -> 67.7 us  [long_filter(): result, unused = lax.scan(scan_step, initial, (stacked, starts))]
where the time goes in v1:
time: 845 us; the launch traced here: 833 us
  waiting for transfers between devices  379 us (45%)
  matrix products  243 us (29%)
  local copies, waits for them, and re-layouts  117 us (14%)
  other arithmetic  54.1 us (6%)
  starting transfers between devices  23.3 us (3%)
  blocking collectives  14 us (2%)
    all_to_all x1, waiting for transfers between devices, long_filter(): jax.lax.all_to_all(arr_now, axis_name='ctx', split_axis=0, concat_axis=0)  358 us
    dot_general x32, matrix products, filter_tile(): jnp.einsum('ejz,ejx->ezx', left_neighbor, right_neighbor, precision=lax.P...  119 us
    dot_general x32, matrix products, split_product(): jnp.einsum(form, lower_part, inputs, preferred_element_type=jnp.float32)  100 us
    dynamic_slice x64, local copies, waits for them, and re-layouts, long_filter(): result, unused = lax.scan(scan_step, initial, (stacked, starts))  67.7 us
    unnamed x13, local copies, waits for them, and re-layouts  28.1 us
    dot_general x32, matrix products, split_product(): jnp.einsum(form, upper_part, inputs, preferred_element_type=jnp.float32)  24.1 us
    sub x32, other arithmetic, filter_tile(): span - in_offsets  21.8 us
    sub x32, other arithmetic, filter_tile(): out_index - piece_start  21.7 us
  transfers between devices with their start and end apart: 3, of which 3 were waited for; matrix products, arithmetic and copies ran while one was open for 0% of the time, Pallas kernels for 0%

profile of v1, /device:TPU:8, one launch (start us, length us, event | category | flops | bytes accessed | tf_op | source)
XLA Modules:
  0.0 833.3 jit_solution(14120530805532378818)
XLA Ops:
  0.0 10.6 %copy.24 = bf16[32,3,8192]{0,1,2:T(4,128)(2,1)} copy(bf16[32,3,8192]{2,0,1:T(8,128)(2,1)} %param.7) | data formatting | bytes 3145728 | tf_op args[0]
  10.6 9.8 %reshape.116 = bf16[8,2,49152]{2,1,0:T(2,128)(2,1)} reshape(bf16[8192,3,32]{2,1,0:T(4,128)(2,1)} %bitcast.55) | data formatting | bytes 3145728
  20.4 5.9 all-to-all-start
  28.5 19.6 %all-to-all-done = bf16[8,2,49152]{2,1,0:T(2,128)(2,1)S(1)} async-done(((bf16[8,2,49152]{2,1,0:T(2,128)(2,1)}), bf16[8,2,49152]{2,1,0:T(2,128)(2,1)S(1)}, u32[]{:S(2)}, u32[]{:S(2)}) %all-to-all-start) | async-done | bytes 1572896 | tf_op jit(solution)/shard_map/all_to_all | solution.py:92
  48.1 7.6 reshape.117
  55.7 10.5 %copy.32 = bf16[32,3,8,1024]{3,0,2,1:T(8,128)(2,1)S(1)} copy(bf16[32,3,8,1024]{0,1,3,2:T(4,128)(2,1)} %bitcast.54) | data formatting | bytes 3145728 | tf_op jit(solution)/shard_map/all_to_all | solution.py:92
  68.4 3.9 multiply_add_fusion
  73.8 5.9 stack.2
  79.7 16.2 %all-to-all-start.1 = ((bf16[32,256,1024]{1,2,0:T(8,128)(2,1)}), bf16[32,256,1024]{1,2,0:T(8,128)(2,1)}, u32[]{:S(2)}, u32[]{:S(2)}) async-start(bf16[32,256,1024]{1,2,0:T(8,128)(2,1)} %stack.2), calls=%async_computation.1 | async-start | bytes 33554432 | tf_op jit(solution)/shard_map/all_to_all | solution.py:76
  96.0 358.3 %all-to-all-done.1 = bf16[32,256,1024]{1,2,0:T(8,128)(2,1)} async-done(((bf16[32,256,1024]{1,2,0:T(8,128)(2,1)}), bf16[32,256,1024]{1,2,0:T(8,128)(2,1)}, u32[]{:S(2)}, u32[]{:S(2)}) %all-to-all-start.1) | async-done | bytes 16777248 | tf_op jit(solution)/shard_map/all_to_all | solution.py:76
  454.2 360.9 %while.13 = (s32[]{:T(128)}, f32[256,16,64]{0,2,1:T(8,128)S(1)}, bf16[32,256,1024]{1,2,0:T(8,128)(2,1)}, s32[32]{0:T(128)S(1)}, f32[16,16]{1,0:T(8,128)S(1)}, /*...) while((s32[]{:T(128)}, f32[256,16,64]{0,2,1:T(8,128)S(1)}, ...), condition=%wide.region_3.4_spmd.clone, body=%wide.region_2.3_spmd.clone.sunk | while | flops 477169920 | bytes 35856544 | solution.py:86
  455.6 3.7 fusion.43
  462.4 3.1 fusion.45
  466.9 3.7 fusion.43
  478.1 3.7 fusion.43
  484.9 3.1 fusion.45
  489.4 3.7 fusion.43
  496.2 3.1 fusion.45
  500.7 3.7 fusion.43
  507.5 3.1 fusion.45
  512.0 3.7 fusion.43
  518.8 3.1 fusion.45
  523.2 3.7 fusion.43
  530.0 3.1 fusion.45
  534.5 3.7 fusion.43
  541.3 3.1 fusion.45
  545.8 3.7 fusion.43
  552.6 3.1 fusion.45
  557.1 3.7 fusion.43
  563.9 3.1 fusion.45
  568.4 3.7 fusion.43
  575.2 3.1 fusion.45
  579.6 3.7 fusion.43
  590.9 3.7 fusion.43
  597.7 3.1 fusion.45
  602.2 3.7 fusion.43
  613.5 3.7 fusion.43
  620.3 3.1 fusion.45
  624.8 3.7 fusion.43
  636.0 3.7 fusion.43
  642.8 3.1 fusion.45
  647.3 3.7 fusion.43
  658.6 3.7 fusion.43
  665.4 3.1 fusion.45
  669.9 3.7 fusion.43
  681.2 3.7 fusion.43
  688.0 3.1 fusion.45
  692.4 3.7 fusion.43
  703.7 3.7 fusion.43
  710.5 3.1 fusion.45
  715.0 3.7 fusion.43
  726.3 3.7 fusion.43
  733.1 3.1 fusion.45
  737.6 3.7 fusion.43
  748.8 3.7 fusion.43
  755.6 3.1 fusion.45
  760.1 3.7 fusion.43
  771.4 3.7 fusion.43
  778.2 3.1 fusion.45
  782.7 3.7 fusion.43
  794.0 3.7 fusion.43
  800.8 3.1 fusion.45
  805.2 3.7 fusion.43
  818.5 14.0 %all_to_all.39 = bf16[8,32,1024]{2,1,0:T(8,128)(2,1)S(1)} all-to-all(bf16[8,32,1024]{2,1,0:T(8,128)(2,1)S(1)} %multiply_convert_fusion), channel_id=1, replica_groups=mesh['ctx'=32,'mp'=8] {'mp'}, dimensions={0} | all-to-all | bytes 1048576 | tf_op jit(solution)/shard_map/all_to_all | solution.py:112
  (301 shorter events, 186.3 us)
Async XLA Ops:
  20.4 5.9 copy-start.3
  20.4 27.7 %all-to-all-start = ((bf16[8,2,49152]{2,1,0:T(2,128)(2,1)}), bf16[8,2,49152]{2,1,0:T(2,128)(2,1)S(1)}, u32[]{:S(2)}, u32[]{:S(2)}) async-start(bf16[8,2,49152]{2,1,0:T(2,128)(2,1)} %reshape.116), calls=%async_computation | async-start | bytes 3145728 | tf_op jit(solution)/shard_map/all_to_all | solution.py:92
  66.3 2.2 collective-permute-start
  79.7 16.2 %copy-start.1 = (f32[16,16]{1,0:T(8,128)S(1)}, f32[16,16]{1,0:T(8,128)}, u32[]{:S(2)}) copy-start(f32[16,16]{1,0:T(8,128)} %param.10) | copy-start | bytes 3076
  79.7 16.2 %copy-start.2 = (f32[16,16]{1,0:T(8,128)S(1)}, f32[16,16]{1,0:T(8,128)}, u32[]{:S(2)}) copy-start(f32[16,16]{1,0:T(8,128)} %param.9) | copy-start | bytes 3076
  79.7 374.5 %all-to-all-start.1 = ((bf16[32,256,1024]{1,2,0:T(8,128)(2,1)}), bf16[32,256,1024]{1,2,0:T(8,128)(2,1)}, u32[]{:S(2)}, u32[]{:S(2)}) async-start(bf16[32,256,1024]{1,2,0:T(8,128)(2,1)} %stack.2), calls=%async_computation.1 | async-start | bytes 33554432 | tf_op jit(solution)/shard_map/all_to_all | solution.py:76
  459.3 2.3 copy-start
  470.6 2.3 copy-start
  481.9 2.3 copy-start
  493.1 2.3 copy-start
  504.4 2.3 copy-start
  515.7 2.3 copy-start
  527.0 2.3 copy-start
  538.3 2.3 copy-start
  549.5 2.3 copy-start
  560.8 2.3 copy-start
  572.1 2.3 copy-start
  583.4 2.3 copy-start
  594.7 2.3 copy-start
  605.9 2.3 copy-start
  617.2 2.3 copy-start
  628.5 2.3 copy-start
  639.8 2.3 copy-start
  651.1 2.3 copy-start
  662.3 2.3 copy-start
  673.6 2.3 copy-start
  684.9 2.3 copy-start
  696.2 2.3 copy-start
  707.5 2.3 copy-start
  718.7 2.3 copy-start
  730.0 2.3 copy-start
  741.3 2.3 copy-start
  752.6 2.3 copy-start
  763.9 2.3 copy-start
  775.1 2.3 copy-start
  786.4 2.3 copy-start
  797.7 2.3 copy-start
  809.0 2.3 copy-start
